TPU v7x, 512 devices: a whole 4x8x8 slice. The times are simulated.
512 devices in a mesh: resp: 64 (over y_lo, z, core), mp: 8 (over y_hi, x).
Axes of the slice: x: 4, y: 8 (y_hi: 2, y_lo: 4; y = y_hi * 4 + y_lo), z: 8, core: 2. Of those that a mesh axis runs over, the one named last changes fastest.
Arguments:
- queries: bfloat16 [16384, 64, 128], P('resp', 'mp'), may hold values from -200 to 200
- response_kv: bfloat16 [16384, 2, 8, 128], P('resp', None, 'mp'), may hold values from -6 to 6
- prefix_kv: bfloat16 [4096, 2, 8, 128], P(('resp', 'mp')), may hold values from -8 to 8
- lengths: int32 [64], P('resp'), may hold values from 128 to 256, as said below
- score_weight: float32 [8192], P('mp'), may hold values from -30 to 30
Outputs:
- attended: bfloat16 [16384, 8192], P('resp', 'mp')
- score: float32 [64], P('resp')
Inputs may be any that keep to these rules, and one draw needn't show every extreme that they name: `lengths`: every length is a multiple of 128; some response is full and some has one tile.
All inputs are finite; a program needn't handle non-finite values.
Results may differ from a plain program's by a relative error of at most 0.0045.
Values may be sent and summed in bfloat16 or wider, within the bound.
No kernel may reach another device: no remote copies, remote signals or barrier semaphores. Data moves between devices by JAX's collectives and lax.ppermute only.
A program may use at most 64 MiB of HBM per device.

v0:
```python
import math
import jax
import jax.numpy as jnp
from jax import lax
from jax.sharding import PartitionSpec as P

neg_large = -1e30


def absorb(carry, keys, values, grouped, factor):
    best, total, accum = carry
    scores = jnp.einsum("grd,sgd->grs", grouped, keys, preferred_element_type=jnp.float32) * factor
    fresh = jnp.maximum(best, jnp.max(scores, axis=-1, keepdims=True))
    shrink = jnp.exp(best - fresh)
    weights = jnp.exp(scores - fresh)
    total = total * shrink + jnp.sum(weights, axis=-1, keepdims=True)
    accum = accum * shrink + jnp.einsum(
        "grs,sgd->grd", weights.astype(jnp.bfloat16), values, preferred_element_type=jnp.float32
    )
    return (fresh, total, accum)


def sweep(carry, whole_cache, grouped, factor):
    count = whole_cache.shape[0]
    block_len = math.gcd(count, 512)
    blocks = whole_cache.reshape((count // block_len, block_len) + whole_cache.shape[1:])

    def one_block(state, block):
        return (absorb(state, block[:, 0], block[:, 1], grouped, factor), None)

    carry, unused = lax.scan(one_block, carry, blocks)
    return carry


def per_device(queries, response_kv, prefix_kv, lengths, score_weight):
    resp_len = queries.shape[0]
    local_heads = queries.shape[1]
    head_size = queries.shape[2]
    local_kv = response_kv.shape[2]
    group = local_heads // local_kv
    rows = group * resp_len
    factor = 1.0 / math.sqrt(head_size)
    length = lengths[0]
    grouped = jnp.transpose(
        queries.reshape(resp_len, local_kv, group, head_size), (1, 2, 0, 3)
    ).reshape(local_kv, rows, head_size)
    key_pos = jnp.arange(resp_len, dtype=jnp.int32)[None, :]
    query_pos = (jnp.arange(rows, dtype=jnp.int32) % resp_len)[:, None]
    allowed = ((key_pos <= query_pos) & (key_pos < length))[None]
    near = (
        jnp.einsum("grd,sgd->grs", grouped, response_kv[:, 0], preferred_element_type=jnp.float32)
        * factor
    )
    near = jnp.where(allowed, near, neg_large)
    best = jnp.max(near, axis=-1, keepdims=True)
    near_w = jnp.where(allowed, jnp.exp(near - best), 0.0)
    total = jnp.sum(near_w, axis=-1, keepdims=True)
    accum = jnp.einsum(
        "grs,sgd->grd",
        near_w.astype(jnp.bfloat16),
        response_kv[:, 1],
        preferred_element_type=jnp.float32,
    )
    start_state = (best, total, accum)
    mine = lax.all_to_all(prefix_kv, "mp", split_axis=2, concat_axis=0, tiled=True)
    collected = lax.all_gather(mine, "resp", axis=0, tiled=True)
    best, total, accum = sweep(start_state, collected, grouped, factor)
    mixed = (accum / total).reshape(local_kv, group, resp_len, head_size)
    mixed = jnp.transpose(mixed, (2, 0, 1, 3)).reshape(resp_len, local_heads * head_size)
    live = jnp.arange(resp_len, dtype=jnp.int32)[:, None] < length
    attended = jnp.where(live, mixed, 0.0).astype(jnp.bfloat16)
    partial_score = jnp.sum(attended.astype(jnp.float32) * score_weight[None, :])
    summed = lax.psum(partial_score, "mp")
    score = (summed / length.astype(jnp.float32)).reshape(1)
    return (attended, score)


def solution(mesh):
    in_specs = (
        P("resp", "mp", None),
        P("resp", None, "mp", None),
        P(("resp", "mp"), None, None, None),
        P("resp"),
        P("mp"),
    )
    out_specs = (P("resp", "mp"), P("resp"))
    return jax.shard_map(
        per_device, mesh=mesh, in_specs=in_specs, out_specs=out_specs, check_vma=False
    )
```

profile of v0, /device:TPU:8, one launch (start us, length us, event | category | flops | bytes accessed | tf_op | source)
XLA Modules:
  0.0 215.8 jit_solution(12020379419026221911)
XLA Ops:
  7.2 0.0 all-gather.2.cloned.1.call-start
  7.2 0.8 copy.18
  8.0 18.6 %all_to_all.18 = bf16[8,2,8,128]{3,0,1,2:T(8,128)(2,1)S(1)} all-to-all(bf16[8,2,8,128]{3,0,1,2:T(8,128)(2,1)S(1)} %copy.18), channel_id=1, replica_groups=mesh['resp'=64,'mp'=8] {'mp'}, dimensions={2} | all-to-all | bytes 65536 | tf_op jit(solution)/shard_map/all_to_all | solution.py:65
  26.6 0.6 copy.35
  27.9 1.1 copy.15
  29.0 1.2 fusion.24
  30.2 0.7 fusion.25
  31.0 0.7 fusion.12
  31.7 1.0 convolution_bitcast_fusion.1
  32.6 110.5 %all-gather.2.cloned.1.call-done = bf16[4096,2,1,128]{3,0,1,2:T(8,128)(2,1)} async-done(((bf16[64,2,1,128]{3,0,1,2:T(8,128)(2,1)}), bf16[4096,2,1,128]{3,0,1,2:T(8,128)(2,1)}) %all-gather.2.cloned.1.call-update) | async-done | bytes 2097168 | tf_op jit(solution)/shard_map/all_gather | solution.py:66
  143.2 29.5 %while.14 = (s32[]{:T(128)}, f32[1,2048,1]{1,2,0:T(1,128)S(1)}, f32[1,2048,1]{1,2,0:T(1,128)S(1)}, f32[1,2048,128]{2,1,0:T(8,128)S(1)}, bf16[8,512,2,1,128]{4,1,...) while((s32[]{:T(128)}, f32[1,2048,1]{1,2,0:T(1,128)S(1)}, f32[1,2048,1]{1,2,0:T(1,128)S(1)}, ...), condition=%wide.region_5.6_spmd, body=%wide.region_2.5_spmd.sunk | while | flops 545787904 | bytes 16121945 | solution.py:31
  143.2 1.0 dynamic-slice_bitcast_fusion.2
  144.2 0.7 multiply_reduce_fusion.3
  144.9 0.7 fusion.31
  145.7 1.2 fusion.32
  146.9 1.0 dynamic-slice_bitcast_fusion.2
  147.8 0.7 multiply_reduce_fusion.3
  148.6 0.7 fusion.31
  149.3 1.2 fusion.32
  150.6 1.0 dynamic-slice_bitcast_fusion.2
  151.5 0.7 multiply_reduce_fusion.3
  152.3 0.7 fusion.31
  153.0 1.2 fusion.32
  154.2 1.0 dynamic-slice_bitcast_fusion.2
  155.2 0.7 multiply_reduce_fusion.3
  156.0 0.7 fusion.31
  156.7 1.2 fusion.32
  157.9 1.0 dynamic-slice_bitcast_fusion.2
  158.9 0.7 multiply_reduce_fusion.3
  159.7 0.7 fusion.31
  160.4 1.2 fusion.32
  161.6 1.0 dynamic-slice_bitcast_fusion.2
  162.6 0.7 multiply_reduce_fusion.3
  163.3 0.7 fusion.31
  164.1 1.2 fusion.32
  165.3 1.0 dynamic-slice_bitcast_fusion.2
  166.3 0.7 multiply_reduce_fusion.3
  167.0 0.7 fusion.31
  167.8 1.2 fusion.32
  169.0 1.0 dynamic-slice_bitcast_fusion.2
  170.0 0.7 multiply_reduce_fusion.3
  170.7 0.7 fusion.31
  171.5 1.2 fusion.32
  172.7 0.3 broadcast_divide_fusion
  173.0 1.0 multiply_reduce_fusion.1
  174.0 0.3 copy.21
  174.4 31.9 %psum.7 = f32[]{:T(128)} all-reduce(f32[]{:T(128)} %multiply_reduce_fusion.1), channel_id=1, replica_groups=mesh['resp'=64,'mp'=8] {'mp'}, use_global_device_ids=true, to_apply=%region_7.8 | all-reduce | flops 1 | bytes 8 | tf_op jit(solution)/shard_map/psum | solution.py:73
  206.2 1.0 fusion.14
  (29 shorter events, 0.4 us)
Async XLA Ops:
  7.2 136.0 %all-gather.2.cloned.1.call-start = ((), (), s32[]{:S(2)}) async-start(), calls=%async_computation.1 | async-start | bytes 2129920 | tf_op jit(solution)/shard_map/all_gather | solution.py:66
  143.2 29.8 %copy-start = (f32[1024]{0:T(1024)S(1)}, f32[1024]{0:T(1024)}, u32[]{:S(2)}) copy-start(f32[1024]{0:T(1024)} %param.11) | copy-start | bytes 12292
Sparse Core Ops, SparseCore 0:
  27.4 115.7 all-gather.1
where the time goes:
time: 216 us
  waiting for transfers between devices  111 us (51%)
  blocking collectives  50.5 us (23%)
  matrix products  16.9 us (8%)
  between operations  16.5 us (8%)
  local copies, waits for them, and re-layouts  11.9 us (6%)
  other arithmetic  9.04 us (4%)
    all_gather x1, waiting for transfers between devices, per_device(): collected = lax.all_gather(mine, 'resp', axis=0, tiled=True)  111 us
    psum x1, blocking collectives, per_device(): summed = lax.psum(partial_score, 'mp')  31.9 us
    all_to_all x1, blocking collectives, per_device(): lax.all_to_all(prefix_kv, 'mp', split_axis=2, concat_axis=0, tiled=True)  18.6 us
    dot_general x8, matrix products, absorb(): jnp.einsum('grs,sgd->grd', weights.astype(jnp.bfloat16), values, preferre...  9.46 us
    squeeze x8, local copies, waits for them, and re-layouts, sweep(): carry, unused = lax.scan(one_block, carry, blocks)  7.82 us
    dot_general x8, matrix products, absorb(): jnp.einsum('grd,sgd->grs', grouped, keys, preferred_element_type=jnp.floa...  5.75 us
    reduce_sum x8, other arithmetic, absorb(): total = total * shrink + jnp.sum(weights, axis=-1, keepdims=True)  5.68 us
  transfers between devices with their start and end apart: 1, of which 1 were waited for; matrix products, arithmetic and copies ran while one was open for 2% of the time, Pallas kernels for 0%

commit v1 on v0

--- a/solution.py
+++ b/solution.py
@@ -63,7 +63,13 @@
     )
     start_state = (best, total, accum)
     mine = lax.all_to_all(prefix_kv, "mp", split_axis=2, concat_axis=0, tiled=True)
-    collected = lax.all_gather(mine, "resp", axis=0, tiled=True)
+
+    def values_fit(join_dim, vals):
+        z2 = jnp.stack([vals for _ in range(lax.axis_size("resp"))], axis=0)
+        extra = lax.all_to_all(z2, "resp", 0, 0)
+        return jnp.concatenate(extra, axis=join_dim)
+
+    collected = values_fit(0, mine)
     best, total, accum = sweep(start_state, collected, grouped, factor)
     mixed = (accum / total).reshape(local_kv, group, resp_len, head_size)
     mixed = jnp.transpose(mixed, (2, 0, 1, 3)).reshape(resp_len, local_heads * head_size)

time: 216 us -> 155 us (0.72)
  the two profiles are of different devices: /device:TPU:8 before, /device:TPU:56 now
where the time goes in v1:
time: 155 us; the launch traced here: 154 us
  waiting for transfers between devices  49.9 us (32%)
  blocking collectives  45.8 us (30%)
  matrix products  16.9 us (11%)
  starting transfers between devices  14.7 us (9%)
  local copies, waits for them, and re-layouts  14.1 us (9%)
  other arithmetic  9.04 us (6%)
  between operations  3.17 us (2%)
    all_to_all x1, waiting for transfers between devices, values_fit(): extra = lax.all_to_all(z2, 'resp', 0, 0)  49.9 us
    psum x1, blocking collectives, per_device(): summed = lax.psum(partial_score, 'mp')  31.5 us
    all_to_all x1, starting transfers between devices, values_fit(): extra = lax.all_to_all(z2, 'resp', 0, 0)  14.7 us
    all_to_all x1, blocking collectives, per_device(): lax.all_to_all(prefix_kv, 'mp', split_axis=2, concat_axis=0, tiled=True)  14.3 us
    dot_general x8, matrix products, absorb(): jnp.einsum('grs,sgd->grd', weights.astype(jnp.bfloat16), values, preferre...  9.46 us
    squeeze x8, local copies, waits for them, and re-layouts, sweep(): carry, unused = lax.scan(one_block, carry, blocks)  7.82 us
    dot_general x8, matrix products, absorb(): jnp.einsum('grd,sgd->grs', grouped, keys, preferred_element_type=jnp.floa...  5.75 us
    reduce_sum x8, other arithmetic, absorb(): total = total * shrink + jnp.sum(weights, axis=-1, keepdims=True)  5.68 us
  transfers between devices with their start and end apart: 1, of which 1 were waited for; matrix products, arithmetic and copies ran while one was open for 2% of the time, Pallas kernels for 0%

profile of v1, /device:TPU:56, one launch (start us, length us, event | category | flops | bytes accessed | tf_op | source)
XLA Modules:
  0.0 154.0 jit_solution(1761800651339547895)
XLA Ops:
  0.6 0.8 copy.18
  1.4 14.3 %all_to_all.20 = bf16[8,2,8,128]{3,0,1,2:T(8,128)(2,1)S(1)} all-to-all(bf16[8,2,8,128]{3,0,1,2:T(8,128)(2,1)S(1)} %copy.18), channel_id=1, replica_groups=mesh['resp'=64,'mp'=8] {'mp'}, dimensions={2} | all-to-all | bytes 65536 | tf_op jit(solution)/shard_map/all_to_all | solution.py:65
  15.7 1.8 %stack.5 = bf16[64,64,2,1,128]{4,1,2,3,0:T(8,128)(2,1)} broadcast(bf16[64,2,128]{2,0,1:T(8,128)(2,1)S(1)} %bitcast.105), dimensions={1,2,4} | broadcast | bytes 2129920 | tf_op jit(solution)/shard_map/stack | solution.py:68
  17.5 14.7 %all-to-all-start.1 = ((bf16[64,64,2,1,128]{4,1,2,3,0:T(8,128)(2,1)}), bf16[64,64,2,1,128]{4,1,2,3,0:T(8,128)(2,1)}, u32[]{:S(2)}, u32[]{:S(2)}) async-start(bf16[64,64,2,1,128]{4,1,2,3,0:T(8,128)(2,1)} %stack.5), calls=%async_computation.1 | async-start | bytes 4194304 | tf_op jit(solution)/shard_map/all_to_all | solution.py:69
  33.0 0.2 fusion.24
  33.2 0.7 fusion.25
  33.9 0.7 fusion.12
  34.6 1.0 convolution_bitcast_fusion.1
  35.6 49.9 %all-to-all-done.1 = bf16[64,64,2,1,128]{4,1,2,3,0:T(8,128)(2,1)} async-done(((bf16[64,64,2,1,128]{4,1,2,3,0:T(8,128)(2,1)}), bf16[64,64,2,1,128]{4,1,2,3,0:T(8,128)(2,1)}, u32[]{:S(2)}, u32[]{:S(2)}) %all-to-all-start.1) | async-done | bytes 2097184 | tf_op jit(solution)/shard_map/all_to_all | solution.py:69
  85.5 3.1 %copy.20 = bf16[64,64,2,1,128]{4,1,0,2,3:T(8,128)(2,1)} copy(bf16[64,64,2,1,128]{4,1,2,3,0:T(8,128)(2,1)} %all-to-all-done.1) | data formatting | bytes 4194304 | tf_op jit(solution)/shard_map/all_to_all | solution.py:69
  88.6 29.5 %while.14 = (s32[]{:T(128)}, f32[1,2048,1]{1,2,0:T(1,128)S(1)}, f32[1,2048,1]{1,2,0:T(1,128)S(1)}, f32[1,2048,128]{2,1,0:T(8,128)S(1)}, bf16[8,512,2,1,128]{4,1,...) while((s32[]{:T(128)}, f32[1,2048,1]{1,2,0:T(1,128)S(1)}, f32[1,2048,1]{1,2,0:T(1,128)S(1)}, ...), condition=%wide.region_5.6_spmd, body=%wide.region_2.5_spmd.sunk | while | flops 545787904 | bytes 16121945 | solution.py:31
  88.6 1.0 dynamic-slice_bitcast_fusion.2
  89.6 0.7 multiply_reduce_fusion.3
  90.3 0.7 fusion.31
  91.1 1.2 fusion.32
  92.3 1.0 dynamic-slice_bitcast_fusion.2
  93.3 0.7 multiply_reduce_fusion.3
  94.0 0.7 fusion.31
  94.8 1.2 fusion.32
  96.0 1.0 dynamic-slice_bitcast_fusion.2
  97.0 0.7 multiply_reduce_fusion.3
  97.7 0.7 fusion.31
  98.4 1.2 fusion.32
  99.7 1.0 dynamic-slice_bitcast_fusion.2
  100.6 0.7 multiply_reduce_fusion.3
  101.4 0.7 fusion.31
  102.1 1.2 fusion.32
  103.3 1.0 dynamic-slice_bitcast_fusion.2
  104.3 0.7 multiply_reduce_fusion.3
  105.1 0.7 fusion.31
  105.8 1.2 fusion.32
  107.0 1.0 dynamic-slice_bitcast_fusion.2
  108.0 0.7 multiply_reduce_fusion.3
  108.8 0.7 fusion.31
  109.5 1.2 fusion.32
  110.7 1.0 dynamic-slice_bitcast_fusion.2
  111.7 0.7 multiply_reduce_fusion.3
  112.4 0.7 fusion.31
  113.2 1.2 fusion.32
  114.4 1.0 dynamic-slice_bitcast_fusion.2
  115.4 0.7 multiply_reduce_fusion.3
  116.1 0.7 fusion.31
  116.9 1.2 fusion.32
  118.1 0.3 broadcast_divide_fusion
  118.4 1.0 multiply_reduce_fusion.1
  119.4 0.3 copy.22
  119.8 31.5 %psum.7 = f32[]{:T(128)} all-reduce(f32[]{:T(128)} %multiply_reduce_fusion.1), channel_id=1, replica_groups=mesh['resp'=64,'mp'=8] {'mp'}, use_global_device_ids=true, to_apply=%region_7.8 | all-reduce | flops 1 | bytes 8 | tf_op jit(solution)/shard_map/psum | solution.py:79
  151.2 1.0 fusion.14
  (34 shorter events, 0.5 us)
Async XLA Ops:
  17.5 15.3 %copy-start = (bf16[256,8,128]{2,1,0:T(8,128)(2,1)S(1)}, bf16[256,8,128]{2,1,0:T(8,128)(2,1)}, u32[]{:S(2)}) copy-start(bf16[256,8,128]{2,1,0:T(8,128)(2,1)} %param.7) | copy-start | bytes 1572868
  17.5 15.4 %copy-start.1 = (bf16[256,2,1,128]{3,1,2,0:T(2,128)(2,1)S(1)}, bf16[256,2,1,128]{3,1,2,0:T(2,128)(2,1)}, u32[]{:S(2)}) copy-start(bf16[256,2,1,128]{3,1,2,0:T(2,128)(2,1)} %param.8) | copy-start | bytes 393220
  17.5 68.0 %all-to-all-start.1 = ((bf16[64,64,2,1,128]{4,1,2,3,0:T(8,128)(2,1)}), bf16[64,64,2,1,128]{4,1,2,3,0:T(8,128)(2,1)}, u32[]{:S(2)}, u32[]{:S(2)}) async-start(bf16[64,64,2,1,128]{4,1,2,3,0:T(8,128)(2,1)} %stack.5), calls=%async_computation.1 | async-start | bytes 4194304 | tf_op jit(solution)/shard_map/all_to_all | solution.py:69
  88.6 29.8 %copy-start.2 = (f32[1024]{0:T(1024)S(1)}, f32[1024]{0:T(1024)}, u32[]{:S(2)}) copy-start(f32[1024]{0:T(1024)} %param.11) | copy-start | bytes 12292
